TPU v7x, 128 devices: a whole 4x4x4 slice. The times are simulated.
128 devices in a mesh: seq: 16 (over x, y), chan: 8 (over z, core).
Axes of the slice: x: 4, y: 4, z: 4, core: 2. Of those that a mesh axis runs over, the one named last changes fastest.
Arguments:
- hyena_query: bfloat16 [4096, 8192], P('seq', 'chan'), may hold values from -6 to 6
- hyena_key: bfloat16 [4096, 8192], P('seq', 'chan'), may hold values from -6 to 6
- hyena_value: bfloat16 [4096, 8192], P('seq', 'chan'), may hold values from -6 to 6
- bias: float32 [8192], P('chan'), may hold values from 0.5 to 1.5
- groups: int32 [8192], P('chan'), may hold values from 0 to 511
- filters: float32 [512, 4096], P('chan', 'seq'), may hold values from -1.5 to 1.5
- att_queries: bfloat16 [4096, 8192], P('seq', 'chan'), may hold values from -45 to 45
- att_keys: bfloat16 [4096, 8192], P('seq', 'chan'), may hold values from -5 to 5
- block_mask: int32 [32, 32], P('seq'), may hold values from 0 to 1, as said below
Outputs:
- hyena_out: bfloat16 [4096, 8192], P('seq', 'chan')
- attn_out: bfloat16 [4096, 8192], P('seq', 'chan')
Inputs may be any that keep to these rules, and one draw needn't show every extreme that they name: block_mask[i, i] = 1 and block_mask[i, j] = 0 for j > i.
All inputs are finite; a program needn't handle non-finite values.
Results may differ from a plain program's by a relative error of at most 0.014.
Values may be sent and summed in bfloat16 or wider, within the bound.
No kernel may reach another device: no remote copies, remote signals or barrier semaphores. Data moves between devices by JAX's collectives and lax.ppermute only.
A program may use at most 128 MiB of HBM per device.

v0:
```python
import math
import jax
import jax.numpy as jnp
from jax import lax
from jax.sharding import PartitionSpec as P

HD = 128
ABLK = 128
highest = lax.Precision.HIGHEST


def swapped(value, axis, stride):
    mask = 2**stride
    pairs = [(source, source ^ mask) for source in range(lax.axis_size(axis))]
    return lax.ppermute(value, axis, pairs)


def shortened(x):

    def short(part):
        return part.astype(jnp.bfloat16) if part.dtype == jnp.float32 else part

    return jax.tree.map(short, x)


def unit_angle(numer, denom):
    return 2.0 * math.pi / denom * numer.astype(jnp.float32)


def twist(real_part, imag_part, cosine, sine):
    return (real_part * cosine - imag_part * sine, real_part * sine + imag_part * cosine)


def expand_pair(signal, device, rows_dev, length):
    positions = device * rows_dev + jnp.arange(rows_dev, dtype=jnp.int32)
    angles = math.pi / length * positions.astype(jnp.float32)
    values = signal.astype(jnp.float32)
    cosine = jnp.cos(angles)[:, None]
    sine = jnp.sin(angles)[:, None]
    real_part = jnp.stack([values, values * cosine])
    imag_part = jnp.stack([jnp.zeros_like(values), -values * sine])
    return (real_part, imag_part)


def section_twiddle(device, level, rows_dev, sign):
    inner = device % (1 << level) * rows_dev + jnp.arange(rows_dev, dtype=jnp.int32)
    angles = unit_angle(inner, rows_dev << level + 1)
    return (jnp.cos(angles)[:, None], sign * jnp.sin(angles)[:, None])


def forward_section(current, partner, device, level, rows_dev):
    cosine, sine = section_twiddle(device, level, rows_dev, -1.0)
    upper = device >> level & 1 == 1
    diff_re = partner[0] - current[0]
    diff_im = partner[1] - current[1]
    turned_re, turned_im = twist(diff_re, diff_im, cosine, sine)
    return (
        jnp.where(upper, turned_re, current[0] + partner[0]),
        jnp.where(upper, turned_im, current[1] + partner[1]),
    )


def inverse_section(current, partner, device, level, rows_dev):
    cosine, sine = section_twiddle(device, level, rows_dev, 1.0)
    upper = device >> level & 1 == 1
    moved_re = jnp.where(upper, current[0], partner[0])
    moved_im = jnp.where(upper, current[1], partner[1])
    base_re = jnp.where(upper, partner[0], current[0])
    base_im = jnp.where(upper, partner[1], current[1])
    turned_re, turned_im = twist(moved_re, moved_im, cosine, sine)
    factor = jnp.where(upper, -1.0, 1.0)
    return (base_re + factor * turned_re, base_im + factor * turned_im)


def local_dft(real_part, imag_part, rows_dev, sign):
    index = jnp.arange(rows_dev, dtype=jnp.int32)
    angles = unit_angle(index[:, None] * index[None, :] % rows_dev, rows_dev)
    cosine = jnp.cos(angles)
    sine = sign * jnp.sin(angles)

    def apply_matrix(matrix, data):
        return jnp.einsum("km,emc->ekc", matrix, data, precision=highest)

    new_re = apply_matrix(cosine, real_part) - apply_matrix(sine, imag_part)
    new_im = apply_matrix(cosine, imag_part) + apply_matrix(sine, real_part)
    return (new_re, new_im)


def butterfly_conv(mixed, bank, groups):
    rows_dev, channels = mixed.shape
    devices = lax.axis_size("seq")
    length = rows_dev * devices
    bit_count = devices.bit_length() - 1
    device = lax.axis_index("seq")
    top_level = bit_count - 1
    partner_mixed = swapped(mixed, "seq", top_level)
    current = expand_pair(mixed, device, rows_dev, length)
    partner = expand_pair(partner_mixed, jnp.bitwise_xor(device, 1 << top_level), rows_dev, length)
    state = forward_section(current, partner, device, top_level, rows_dev)
    for level in range(top_level - 1, -1, -1):
        received = swapped(shortened(jnp.stack(state)), "seq", level)
        state = forward_section(state, (received[0], received[1]), device, level, rows_dev)
    spec_re, spec_im = local_dft(state[0], state[1], rows_dev, -1.0)
    residue = jnp.zeros((), jnp.int32)
    for level in range(bit_count):
        residue = residue + ((device >> level & 1) << bit_count - 1 - level)
    freq_even = 2 * (residue + devices * jnp.arange(rows_dev, dtype=jnp.int32))
    freqs = jnp.concatenate([freq_even, freq_even + 1])
    lags = jnp.arange(length, dtype=jnp.int32)
    angles = unit_angle(lags[:, None] * freqs[None, :] % (2 * length), 2 * length)
    table_re = jnp.dot(bank, jnp.cos(angles), precision=highest)
    table_im = -jnp.dot(bank, jnp.sin(angles), precision=highest)
    chosen_re = jnp.take(table_re, groups, axis=0).T.reshape(2, rows_dev, channels)
    chosen_im = jnp.take(table_im, groups, axis=0).T.reshape(2, rows_dev, channels)
    prod_re, prod_im = twist(spec_re, spec_im, chosen_re, chosen_im)
    state = local_dft(prod_re, prod_im, rows_dev, 1.0)
    for level in range(bit_count):
        received = swapped(shortened(jnp.stack(state)), "seq", level)
        state = inverse_section(state, (received[0], received[1]), device, level, rows_dev)
    positions = device * rows_dev + jnp.arange(rows_dev, dtype=jnp.int32)
    final_angles = math.pi / length * positions.astype(jnp.float32)
    cosine = jnp.cos(final_angles)[:, None]
    sine = jnp.sin(final_angles)[:, None]
    return (state[0][0] + cosine * state[0][1] - sine * state[1][1]) / (2.0 * length)


def attention(att_queries, att_keys, hyena_out, block_mask):
    rows_dev, channels = att_queries.shape
    head_count = channels // HD
    device = lax.axis_index("seq")
    block_count = block_mask.shape[1]
    queries = att_queries.reshape(rows_dev, head_count, HD)
    mask_rows = jnp.repeat(block_mask, ABLK, axis=0).astype(jnp.float32)
    query_pos = device * rows_dev + jnp.arange(rows_dev, dtype=jnp.int32)
    scale = HD ** (-0.5)
    key_piece = lax.all_gather(att_keys, "seq", axis=0, tiled=True)
    value_piece = lax.all_gather(hyena_out, "seq", axis=0, tiled=True)
    piece_rows = key_piece.shape[0]
    key_pos = jnp.arange(piece_rows, dtype=jnp.int32)
    onehot = (
        jnp.arange(block_count, dtype=jnp.int32)[:, None] == (key_pos // ABLK)[None, :]
    ).astype(jnp.float32)
    allowed = (jnp.dot(mask_rows, onehot, preferred_element_type=jnp.float32) > 0.5) & (
        key_pos[None, :] <= query_pos[:, None]
    )
    keys_here = key_piece.reshape(piece_rows, head_count, HD)
    values_here = value_piece.reshape(piece_rows, head_count, HD)
    scores = (
        jnp.einsum("thd,shd->hts", queries, keys_here, preferred_element_type=jnp.float32) * scale
    )
    scores = jnp.where(allowed[None], scores, -1e30)
    old_max = jnp.full((head_count, rows_dev), -1e30, jnp.float32)
    new_max = jnp.maximum(old_max, jnp.max(scores, axis=-1))
    weights = jnp.where(allowed[None], jnp.exp(scores - new_max[..., None]), 0.0)
    new_total = jnp.sum(weights, axis=-1)
    new_acc = jnp.einsum(
        "hts,shd->htd",
        weights.astype(jnp.bfloat16),
        values_here,
        preferred_element_type=jnp.float32,
    )
    result = new_acc / new_total[..., None]
    return result.transpose(1, 0, 2).reshape(rows_dev, channels).astype(jnp.bfloat16)


def on_device(
    hyena_query, hyena_key, hyena_value, bias, groups, filters, att_queries, att_keys, block_mask
):
    mixed = (hyena_key.astype(jnp.float32) * hyena_value.astype(jnp.float32)).astype(jnp.bfloat16)
    bank = lax.all_gather(filters.astype(jnp.bfloat16), "chan", axis=0, tiled=True).astype(
        filters.dtype
    )
    bank = lax.all_gather(bank.astype(jnp.bfloat16), "seq", axis=1, tiled=True).astype(bank.dtype)
    conv = butterfly_conv(mixed, bank, groups)
    hyena_out = (
        hyena_query.astype(jnp.float32) * (conv + bias[None, :] * mixed.astype(jnp.float32))
    ).astype(jnp.bfloat16)
    attn_out = attention(att_queries, att_keys, hyena_out, block_mask)
    return (hyena_out, attn_out)


def solution(mesh):
    return jax.shard_map(
        on_device,
        mesh=mesh,
        in_specs=(
            P("seq", "chan"),
            P("seq", "chan"),
            P("seq", "chan"),
            P("chan"),
            P("chan"),
            P("chan", "seq"),
            P("seq", "chan"),
            P("seq", "chan"),
            P("seq", None),
        ),
        out_specs=(P("seq", "chan"), P("seq", "chan")),
        check_vma=False,
    )
```

profile of v0, /device:TPU:0, one launch (start us, length us, event | category | flops | bytes accessed | tf_op | source)
XLA Modules:
  0.0 675.8 jit_solution(9191021837587464185)
XLA Ops:
  8.1 15.2 %all_gather.12 = bf16[512,256]{1,0:T(8,128)(2,1)} all-gather(bf16[64,256]{1,0:T(8,128)(2,1)S(1)} %convert_element_type.294), channel_id=1, replica_groups=mesh['seq'=16,'chan'=8] {'chan'}, dimensions={0}, use_global_device_ids=true | all-gather | bytes 294912 | tf_op jit(solution)/shard_map/all_gather | solution.py:170
  27.2 3.0 collective-permute-start
  30.5 14.4 %collective-permute-done = bf16[256,1024]{0,1:T(8,128)(2,1)S(1)} collective-permute-done((bf16[256,1024]{0,1:T(8,128)(2,1)S(1)}, bf16[256,1024]{0,1:T(8,128)(2,1)S(1)}, u32[]{:S(2)}, u32[]{:S(2)}) %collective-permute-start) | collective-permute-done | bytes 524320 | tf_op jit(solution)/shard_map/ppermute | solution.py:15
  45.2 2.2 convert_bitcast_fusion.12
  47.4 1.6 pad_maximum_fusion.2
  49.0 2.0 collective-permute-start.1
  51.0 62.4 %collective-permute-done.1 = bf16[2,2,256,1024]{2,3,1,0:T(8,128)(2,1)} collective-permute-done((bf16[2,2,256,1024]{2,3,1,0:T(8,128)(2,1)}, bf16[2,2,256,1024]{2,3,1,0:T(8,128)(2,1)}, u32[]{:S(2)}, u32[]{:S(2)}) %collective-permute-start.1) | collective-permute-done | bytes 2097184 | tf_op jit(solution)/shard_map/ppermute | solution.py:15
  113.4 5.3 convert_bitcast_fusion.10
  118.9 2.7 collective-permute-start.2
  121.6 45.3 %collective-permute-done.2 = bf16[2,2,256,1024]{2,3,1,0:T(8,128)(2,1)} collective-permute-done((bf16[2,2,256,1024]{2,3,1,0:T(8,128)(2,1)S(1)}, bf16[2,2,256,1024]{2,3,1,0:T(8,128)(2,1)}, u32[]{:S(2)}, u32[]{:S(2)}) %collective-permute-start.2) | collective-permute-done | bytes 2097184 | tf_op jit(solution)/shard_map/ppermute | solution.py:15
  166.9 5.3 convert_bitcast_fusion.8
  173.7 2.0 copy.32
  176.1 62.9 %collective-permute-done.3 = bf16[2,2,256,1024]{2,3,1,0:T(8,128)(2,1)} collective-permute-done((bf16[2,2,256,1024]{2,3,1,0:T(8,128)(2,1)}, bf16[2,2,256,1024]{2,3,1,0:T(8,128)(2,1)}, u32[]{:S(2)}, u32[]{:S(2)}) %collective-permute-start.3) | collective-permute-done | bytes 2097184 | tf_op jit(solution)/shard_map/ppermute | solution.py:15
  239.1 3.2 fusion.26
  242.3 2.8 fusion.84
  245.2 4.2 fusion.82
  249.4 4.2 convolution_subtract_fusion.1
  253.6 48.3 %fusion.37 = f32[512,512]{0,1:T(8,128)S(1)} fusion(bf16[512,4096]{1,0:T(8,128)(2,1)} %all-gather.4.cloned.1.call-done, s32[512]{0:T(512)S(1)} %pad_add_fusion.1), kind=kOutput, calls=%fused_computation.100 | convolution fusion | flops 12914262016 | bytes 5244928 | tf_op jit(solution)/shard_map/dot_general | solution.py:111
  302.2 49.3 %fusion.46 = f32[512,512]{0,1:T(8,128)} fusion(bf16[512,4096]{1,0:T(8,128)(2,1)} %all-gather.4.cloned.1.call-done, s32[512]{0:T(512)S(1)} %pad_add_fusion.1), kind=kOutput, calls=%fused_computation.103 | convolution fusion | flops 12914524160 | bytes 5244928 | tf_op jit(solution)/shard_map/dot_general | solution.py:112
  351.5 1.6 copy.26
  353.1 4.9 gather_fusion.1
  358.0 4.9 gather_fusion
  362.9 4.0 select_bitcast_fusion
  366.8 2.9 copy.27
  369.7 2.9 copy.28
  372.7 1.9 copy.24
  374.5 3.2 copy.25
  377.8 6.5 fusion.34
  384.3 2.8 fusion.86
  387.1 2.9 convolution_add_fusion
  390.1 2.8 fusion.88
  393.0 3.1 convolution_subtract_fusion
  399.2 39.0 %collective-permute-done.4 = bf16[2,2,256,1024]{2,3,1,0:T(8,128)(2,1)} collective-permute-done((bf16[2,2,256,1024]{2,3,1,0:T(8,128)(2,1)}, bf16[2,2,256,1024]{2,3,1,0:T(8,128)(2,1)}, u32[]{:S(2)}, u32[]{:S(2)}) %collective-permute-start.4) | collective-permute-done | bytes 2097184 | tf_op jit(solution)/shard_map/ppermute | solution.py:15
  438.1 5.5 convert_bitcast_fusion.7
  443.6 1.6 pad_maximum_fusion.6
  445.2 39.0 %collective-permute-done.5 = bf16[2,2,256,1024]{2,3,1,0:T(8,128)(2,1)} collective-permute-done((bf16[2,2,256,1024]{2,3,1,0:T(8,128)(2,1)}, bf16[2,2,256,1024]{2,3,1,0:T(8,128)(2,1)}, u32[]{:S(2)}, u32[]{:S(2)}) %collective-permute-start.5) | collective-permute-done | bytes 2097184 | tf_op jit(solution)/shard_map/ppermute | solution.py:15
  484.3 5.4 convert_bitcast_fusion.5
  490.0 39.7 %collective-permute-done.6 = bf16[2,2,256,1024]{2,3,1,0:T(8,128)(2,1)} collective-permute-done((bf16[2,2,256,1024]{2,3,1,0:T(8,128)(2,1)S(1)}, bf16[2,2,256,1024]{2,3,1,0:T(8,128)(2,1)}, u32[]{:S(2)}, u32[]{:S(2)}) %collective-permute-start.6) | collective-permute-done | bytes 2097184 | tf_op jit(solution)/shard_map/ppermute | solution.py:15
  529.7 5.4 convert_bitcast_fusion.3
  535.1 1.6 pad_maximum_fusion.8
  536.7 2.0 copy.20
  538.7 31.9 %collective-permute-done.7 = bf16[2,2,256,1024]{2,3,1,0:T(8,128)(2,1)} collective-permute-done((bf16[2,2,256,1024]{2,3,1,0:T(8,128)(2,1)}, bf16[2,2,256,1024]{2,3,1,0:T(8,128)(2,1)}, u32[]{:S(2)}, u32[]{:S(2)}) %collective-permute-start.7) | collective-permute-done | bytes 2097184 | tf_op jit(solution)/shard_map/ppermute | solution.py:15
  572.1 2.4 fusion.33
  577.3 2.7 copy.31
  580.0 18.4 %fusion = (f32[8,256]{1,0:T(8,128)S(1)}, f32[8,256,4096]{2,1,0:T(8,128)}) fusion(pred[256,4096]{1,0:T(8,128)(4,1)S(1)} %copy.31, bf16[4096,8,128]{0,2,1:T(8,128)(2,1)} %bitcast.287, bf16[256,1024]{1,0:T(8,128)(2,1)S(1)} %copy-done), kind=kOutput, calls=%fused_computation.4 | convolution fusion | flops 2172647424 | bytes 43524096 | tf_op jit(solution)/shard_map/thd,shd->hts/dot_general | solution.py:149
  598.4 16.4 %fusion.1 = f32[8,256]{1,0:T(8,128)S(1)} fusion(f32[8,256,4096]{2,1,0:T(8,128)} %get-tuple-element.57, f32[8,256]{1,0:T(8,128)S(1)} %broadcast_maximum_fusion, pred[256,4096]{1,0:T(8,128)(4,1)S(1)} %copy.31), kind=kLoop, calls=%fused_computation.5 | loop fusion | flops 41940992 | bytes 34619392 | tf_op jit(solution)/shard_map/reduce_sum | solution.py:155
  615.9 35.7 %all-gather.8.cloned.1.call-done = bf16[4096,1024]{0,1:T(8,128)(2,1)} async-done(((bf16[256,1024]{0,1:T(8,128)(2,1)}), bf16[4096,1024]{0,1:T(8,128)(2,1)}) %all-gather.8.cloned.1.call-update) | async-done | bytes 8388624 | tf_op jit(solution)/shard_map/all_gather | solution.py:137
  651.6 16.3 %divide_convert_fusion = bf16[256,8,128]{0,2,1:T(8,128)(2,1)S(1)} fusion(bf16[4096,8,128]{0,2,1:T(8,128)(2,1)} %bitcast.293, f32[8,256,4096]{2,1,0:T(8,128)} %get-tuple-element.57, f32[8,256]{1,0:T(8,128)S(1)} %broadcast_maximum_fusion, pred[256,4096]{1,0:T(8,128)(4,1)S(1)} %copy.31, f32[256,8]{0,1:T(8,128)S(1)} %bitcast.292), kind=kOutput, calls=%fused_computation.144 | convolution fusion | flops 2189950976 | bytes 43532288 | tf_op jit(solution)/shard_map/hts,shd->htd/dot_general | solution.py:156
  (77 shorter events, 17.4 us)
Async XLA Ops:
  7.2 572.8 %copy-start = (bf16[256,1024]{1,0:T(8,128)(2,1)S(1)}, bf16[256,1024]{1,0:T(8,128)(2,1)}, u32[]{:S(2)}) copy-start(bf16[256,1024]{1,0:T(8,128)(2,1)} %param.17) | copy-start | bytes 1572868
  7.2 246.4 %all-gather.4.cloned.1.call-start = ((), (), s32[]{:S(2)}) async-start(), calls=%async_computation | async-start | bytes 4456448 | tf_op jit(solution)/shard_map/all_gather | solution.py:173
  23.4 556.6 %all-gather.6.cloned.1.call-start = ((), (), s32[]{:S(2)}) async-start(), calls=%async_computation.1 | async-start | bytes 8912896 | tf_op jit(solution)/shard_map/all_gather | solution.py:136
  27.2 17.8 %collective-permute-start = (bf16[256,1024]{0,1:T(8,128)(2,1)S(1)}, bf16[256,1024]{0,1:T(8,128)(2,1)S(1)}, u32[]{:S(2)}, u32[]{:S(2)}) collective-permute-start(bf16[256,1024]{0,1:T(8,128)(2,1)S(1)} %get-tuple-element.34), channel_id=1, source_target_pairs={{0,64},{8,72},{16,80},{24,88},{32,96},{40,104},{48,112},{56,120},{... | collective-permute-start | bytes 1572872 | tf_op jit(solution)/shard_map/ppermute | solution.py:15
  30.5 14.7 %copy-start.7 = (f32[1,256,1024]{1,2,0:T(8,128)S(1)}, f32[1,256,1024]{1,2,0:T(8,128)}, u32[]{:S(2)}) copy-start(f32[1,256,1024]{1,2,0:T(8,128)} %get-tuple-element.33) | copy-start | bytes 3145732
  49.0 64.4 %collective-permute-start.1 = (bf16[2,2,256,1024]{2,3,1,0:T(8,128)(2,1)}, bf16[2,2,256,1024]{2,3,1,0:T(8,128)(2,1)}, u32[]{:S(2)}, u32[]{:S(2)}) collective-permute-start(bf16[2,2,256,1024]{2,3,1,0:T(8,128)(2,1)} %pad_maximum_fusion.2), channel_id=1, source_target_pairs={{0,32},{8,40},{16,48},{24,56},{32,0},{40,8},{48,16},{56,24},{64,96... | collective-permute-start | bytes 6291464 | tf_op jit(solution)/shard_map/ppermute | solution.py:15
  118.9 48.0 %collective-permute-start.2 = (bf16[2,2,256,1024]{2,3,1,0:T(8,128)(2,1)S(1)}, bf16[2,2,256,1024]{2,3,1,0:T(8,128)(2,1)}, u32[]{:S(2)}, u32[]{:S(2)}) collective-permute-start(bf16[2,2,256,1024]{2,3,1,0:T(8,128)(2,1)S(1)} %pad_maximum_fusion.3), channel_id=1, source_target_pairs={{0,16},{8,24},{16,0},{24,8},{32,48},{40,56},{48,32},{56,40},{64,80... | collective-permute-start | bytes 6291464 | tf_op jit(solution)/shard_map/ppermute | solution.py:15
  172.2 3.9 copy-start.9
  173.7 65.4 %collective-permute-start.3 = (bf16[2,2,256,1024]{2,3,1,0:T(8,128)(2,1)}, bf16[2,2,256,1024]{2,3,1,0:T(8,128)(2,1)}, u32[]{:S(2)}, u32[]{:S(2)}) collective-permute-start(bf16[2,2,256,1024]{2,3,1,0:T(8,128)(2,1)} %pad_maximum_fusion.4), channel_id=1, source_target_pairs={{0,8},{8,0},{16,24},{24,16},{32,40},{40,32},{48,56},{56,48},{64,72... | collective-permute-start | bytes 6291464 | tf_op jit(solution)/shard_map/ppermute | solution.py:15
  175.8 475.8 %all-gather.8.cloned.1.call-start = ((), (), s32[]{:S(2)}) async-start(), calls=%async_computation.2 | async-start | bytes 8912896 | tf_op jit(solution)/shard_map/all_gather | solution.py:137
  242.3 2.9 copy-start.1
  374.5 3.2 copy-start.2
  396.1 1.4 copy-start.3
  399.1 39.0 %collective-permute-start.4 = (bf16[2,2,256,1024]{2,3,1,0:T(8,128)(2,1)}, bf16[2,2,256,1024]{2,3,1,0:T(8,128)(2,1)}, u32[]{:S(2)}, u32[]{:S(2)}) collective-permute-start(bf16[2,2,256,1024]{2,3,1,0:T(8,128)(2,1)} %pad_maximum_fusion.5), channel_id=1, source_target_pairs={{0,8},{8,0},{16,24},{24,16},{32,40},{40,32},{48,56},{56,48},{64,72... | collective-permute-start | bytes 6291464 | tf_op jit(solution)/shard_map/ppermute | solution.py:15
  443.6 40.6 %copy-start.5 = (f32[2,256,1024]{1,2,0:T(8,128)S(1)}, f32[2,256,1024]{1,2,0:T(8,128)}, u32[]{:S(2)}) copy-start(f32[2,256,1024]{1,2,0:T(8,128)} %get-tuple-element.18) | copy-start | bytes 6291460
  445.2 39.1 %collective-permute-start.5 = (bf16[2,2,256,1024]{2,3,1,0:T(8,128)(2,1)}, bf16[2,2,256,1024]{2,3,1,0:T(8,128)(2,1)}, u32[]{:S(2)}, u32[]{:S(2)}) collective-permute-start(bf16[2,2,256,1024]{2,3,1,0:T(8,128)(2,1)} %pad_maximum_fusion.6), channel_id=1, source_target_pairs={{0,16},{8,24},{16,0},{24,8},{32,48},{40,56},{48,32},{56,40},{64,80... | collective-permute-start | bytes 6291464 | tf_op jit(solution)/shard_map/ppermute | solution.py:15
  489.8 39.9 %collective-permute-start.6 = (bf16[2,2,256,1024]{2,3,1,0:T(8,128)(2,1)S(1)}, bf16[2,2,256,1024]{2,3,1,0:T(8,128)(2,1)}, u32[]{:S(2)}, u32[]{:S(2)}) collective-permute-start(bf16[2,2,256,1024]{2,3,1,0:T(8,128)(2,1)S(1)} %pad_maximum_fusion.7), channel_id=1, source_target_pairs={{0,32},{8,40},{16,48},{24,56},{32,0},{40,8},{48,16},{56,24},{64,96... | collective-permute-start | bytes 6291464 | tf_op jit(solution)/shard_map/ppermute | solution.py:15
  536.7 34.0 %collective-permute-start.7 = (bf16[2,2,256,1024]{2,3,1,0:T(8,128)(2,1)}, bf16[2,2,256,1024]{2,3,1,0:T(8,128)(2,1)}, u32[]{:S(2)}, u32[]{:S(2)}) collective-permute-start(bf16[2,2,256,1024]{2,3,1,0:T(8,128)(2,1)} %pad_maximum_fusion.8), channel_id=1, source_target_pairs={{0,64},{8,72},{16,80},{24,88},{32,96},{40,104},{48,112},{56,120},{... | collective-permute-start | bytes 6291464 | tf_op jit(solution)/shard_map/ppermute | solution.py:15
  538.7 33.4 %copy-start.4 = (f32[2,256,1024]{1,2,0:T(8,128)S(1)}, f32[2,256,1024]{1,2,0:T(8,128)}, u32[]{:S(2)}) copy-start(f32[2,256,1024]{1,2,0:T(8,128)} %get-tuple-element.10) | copy-start | bytes 6291460
  572.1 2.4 copy-start.8
  572.1 2.4 copy-start.10
  574.5 1.5 copy-start.11
  598.4 16.4 %copy-start.6 = (bf16[256,1024]{0,1:T(8,128)(2,1)S(1)}, bf16[256,1024]{0,1:T(8,128)(2,1)}, u32[]{:S(2)}) copy-start(bf16[256,1024]{0,1:T(8,128)(2,1)} %fusion.57) | copy-start | bytes 1572868
Sparse Core Ops, SparseCore 0:
  23.5 73.5 all-gather.3
  175.9 90.3 all-gather.5
  576.1 75.4 all-gather.7
where the time goes:
time: 682 us; the launch traced here: 676 us
  waiting for transfers between devices  370 us (54%)
  matrix products  163 us (24%)
  other arithmetic  69.2 us (10%)
  local copies, waits for them, and re-layouts  35.3 us (5%)
  blocking collectives  15.2 us (2%)
  between operations  14.6 us (2%)
  starting transfers between devices  8.07 us (1%)
    ppermute x8, waiting for transfers between devices, swapped(): return lax.ppermute(value, axis, pairs)  335 us
    dot_general x1, matrix products, butterfly_conv(): table_im = -jnp.dot(bank, jnp.sin(angles), precision=highest)  49.3 us
    dot_general x1, matrix products, butterfly_conv(): table_re = jnp.dot(bank, jnp.cos(angles), precision=highest)  48.3 us
    another operation x15, other arithmetic, butterfly_conv(): received = swapped(shortened(jnp.stack(state)), 'seq', level)  37.4 us
    all_gather x1, waiting for transfers between devices, attention(): value_piece = lax.all_gather(hyena_out, 'seq', axis=0, tiled=True)  35.7 us
    dot_general x8, matrix products, apply_matrix(): return jnp.einsum('km,emc->ekc', matrix, data, precision=highest)  29.4 us
    dot_general x1, matrix products, attention(): jnp.einsum('thd,shd->hts', queries, keys_here, preferred_element_type=jnp...  18.4 us
    reduce_sum x1, other arithmetic, attention(): new_total = jnp.sum(weights, axis=-1)  16.4 us
  transfers between devices with their start and end apart: 11, of which 9 were waited for; matrix products, arithmetic and copies ran while one was open for 37% of the time, Pallas kernels for 0%

commit v1 on v0

--- a/solution.py
+++ b/solution.py
@@ -134,7 +134,34 @@
     query_pos = device * rows_dev + jnp.arange(rows_dev, dtype=jnp.int32)
     scale = HD ** (-0.5)
     key_piece = lax.all_gather(att_keys, "seq", axis=0, tiled=True)
-    value_piece = lax.all_gather(hyena_out, "seq", axis=0, tiled=True)
+
+    def time_point(slab_in, named_axis):
+        earlier, later, state_now = (
+            lax.axis_size(named_axis),
+            lax.axis_index(named_axis),
+            slab_in.shape[0],
+        )
+        vals = [(idx, (idx + 1) % earlier) for idx in range(earlier)]
+        entries = [(idx, (idx - 1) % earlier) for idx in range(earlier)]
+        mixed_arr = jnp.zeros(
+            (*slab_in.shape[:0], earlier * state_now, *slab_in.shape[1:]), slab_in.dtype
+        )
+        mixed_arr = lax.dynamic_update_slice_in_dim(mixed_arr, slab_in, later * state_now, axis=0)
+        new = w_next = slab_in
+        ready = earlier // 2
+        for p in range(1, ready + 1):
+            new = lax.ppermute(new, named_axis, vals)
+            mixed_arr = lax.dynamic_update_slice_in_dim(
+                mixed_arr, new, (later - p) % earlier * state_now, axis=0
+            )
+            if p < earlier - ready:
+                w_next = lax.ppermute(w_next, named_axis, entries)
+                mixed_arr = lax.dynamic_update_slice_in_dim(
+                    mixed_arr, w_next, (later + p) % earlier * state_now, axis=0
+                )
+        return mixed_arr
+
+    value_piece = time_point(hyena_out, "seq")
     piece_rows = key_piece.shape[0]
     key_pos = jnp.arange(piece_rows, dtype=jnp.int32)
     onehot = (

time: 682 us -> 757 us (1.11)
  starting transfers between devices: 8.07 us -> 48 us
  local copies, waits for them, and re-layouts: 35.3 us -> 60.8 us
  waiting for transfers between devices: 370 us -> 381 us
    ppermute x0 -> x15, waiting for transfers between devices: none -> 46.1 us  [the longest x8 44.7 us: time_point(): new = lax.ppermute(new, named_axis, vals)]
    ppermute x0 -> x15, starting transfers between devices: none -> 40 us  [the longest x7 37 us: time_point(): w_next = lax.ppermute(w_next, named_axis, entries)]
    all_gather x1 -> x0, waiting for transfers between devices: 35.7 us -> none  [attention(): value_piece = lax.all_gather(hyena_out, 'seq', axis=0, tiled=True)]
    dynamic_update_slice x0 -> x15, local copies, waits for them, and re-layouts: none -> 21.4 us  [the longest x7 11.3 us: time_point(): lax.dynamic_update_slice_in_dim(mixed_arr, w_next, (later + p) % earlier...]
  transfers between devices with their start and end apart: 11 -> 25, of which waited for: 9 -> 15; matrix products, arithmetic and copies ran while one was open for 37% -> 36% of each run, Pallas kernels for 0% -> 0%
where the time goes in v1:
time: 757 us; the launch traced here: 750 us
  waiting for transfers between devices  381 us (50%)
  matrix products  163 us (22%)
  other arithmetic  68 us (9%)
  local copies, waits for them, and re-layouts  60.8 us (8%)
  starting transfers between devices  48 us (6%)
  blocking collectives  15.2 us (2%)
  between operations  14.8 us (2%)
    ppermute x8, waiting for transfers between devices, swapped(): return lax.ppermute(value, axis, pairs)  335 us
    dot_general x1, matrix products, butterfly_conv(): table_im = -jnp.dot(bank, jnp.sin(angles), precision=highest)  49.3 us
    dot_general x1, matrix products, butterfly_conv(): table_re = jnp.dot(bank, jnp.cos(angles), precision=highest)  48.3 us
    ppermute x8, waiting for transfers between devices, time_point(): new = lax.ppermute(new, named_axis, vals)  44.7 us
    another operation x15, other arithmetic, butterfly_conv(): received = swapped(shortened(jnp.stack(state)), 'seq', level)  37.2 us
    ppermute x7, starting transfers between devices, time_point(): w_next = lax.ppermute(w_next, named_axis, entries)  37 us
    dot_general x8, matrix products, apply_matrix(): return jnp.einsum('km,emc->ekc', matrix, data, precision=highest)  29.4 us
    dot_general x1, matrix products, attention(): jnp.einsum('thd,shd->hts', queries, keys_here, preferred_element_type=jnp...  18.2 us
  transfers between devices with their start and end apart: 25, of which 15 were waited for; matrix products, arithmetic and copies ran while one was open for 36% of the time, Pallas kernels for 0%

profile of v1, /device:TPU:0, one launch (start us, length us, event | category | flops | bytes accessed | tf_op | source)
XLA Modules:
  0.0 750.3 jit_solution(195048385253374852)
XLA Ops:
  8.1 15.2 %all_gather.9 = bf16[512,256]{1,0:T(8,128)(2,1)} all-gather(bf16[64,256]{1,0:T(8,128)(2,1)S(1)} %convert_element_type.294), channel_id=1, replica_groups=mesh['seq'=16,'chan'=8] {'chan'}, dimensions={0}, use_global_device_ids=true | all-gather | bytes 294912 | tf_op jit(solution)/shard_map/all_gather | solution.py:197
  27.2 3.0 collective-permute-start
  30.5 14.4 %collective-permute-done = bf16[256,1024]{0,1:T(8,128)(2,1)S(1)} collective-permute-done((bf16[256,1024]{0,1:T(8,128)(2,1)S(1)}, bf16[256,1024]{0,1:T(8,128)(2,1)S(1)}, u32[]{:S(2)}, u32[]{:S(2)}) %collective-permute-start) | collective-permute-done | bytes 524320 | tf_op jit(solution)/shard_map/ppermute | solution.py:15
  50.9 62.4 %collective-permute-done.1 = bf16[2,2,256,1024]{2,3,1,0:T(8,128)(2,1)} collective-permute-done((bf16[2,2,256,1024]{2,3,1,0:T(8,128)(2,1)}, bf16[2,2,256,1024]{2,3,1,0:T(8,128)(2,1)}, u32[]{:S(2)}, u32[]{:S(2)}) %collective-permute-start.1) | collective-permute-done | bytes 2097184 | tf_op jit(solution)/shard_map/ppermute | solution.py:15
  113.3 5.3 convert_bitcast_fusion.10
  121.6 45.3 %collective-permute-done.2 = bf16[2,2,256,1024]{2,3,1,0:T(8,128)(2,1)} collective-permute-done((bf16[2,2,256,1024]{2,3,1,0:T(8,128)(2,1)S(1)}, bf16[2,2,256,1024]{2,3,1,0:T(8,128)(2,1)}, u32[]{:S(2)}, u32[]{:S(2)}) %collective-permute-start.2) | collective-permute-done | bytes 2097184 | tf_op jit(solution)/shard_map/ppermute | solution.py:15
  166.9 5.3 convert_bitcast_fusion.8
  176.0 63.1 %collective-permute-done.3 = bf16[2,2,256,1024]{2,3,1,0:T(8,128)(2,1)} collective-permute-done((bf16[2,2,256,1024]{2,3,1,0:T(8,128)(2,1)}, bf16[2,2,256,1024]{2,3,1,0:T(8,128)(2,1)}, u32[]{:S(2)}, u32[]{:S(2)}) %collective-permute-start.3) | collective-permute-done | bytes 2097184 | tf_op jit(solution)/shard_map/ppermute | solution.py:15
  239.1 3.2 fusion.26
  242.4 2.8 fusion.84
  245.2 4.2 fusion.82
  249.4 4.2 convolution_subtract_fusion.1
  253.6 48.3 %fusion.37 = f32[512,512]{0,1:T(8,128)S(1)} fusion(bf16[512,4096]{1,0:T(8,128)(2,1)} %all-gather.3.cloned.1.call-done, s32[512]{0:T(512)S(1)} %pad_add_fusion.1), kind=kOutput, calls=%fused_computation.100 | convolution fusion | flops 12914262016 | bytes 5244928 | tf_op jit(solution)/shard_map/dot_general | solution.py:111
  302.3 49.3 %fusion.46 = f32[512,512]{0,1:T(8,128)} fusion(bf16[512,4096]{1,0:T(8,128)(2,1)} %all-gather.3.cloned.1.call-done, s32[512]{0:T(512)S(1)} %pad_add_fusion.1), kind=kOutput, calls=%fused_computation.103 | convolution fusion | flops 12914524160 | bytes 5244928 | tf_op jit(solution)/shard_map/dot_general | solution.py:112
  353.1 4.9 gather_fusion.1
  358.0 4.9 gather_fusion
  363.0 4.0 select_bitcast_fusion
  367.0 2.9 copy.27
  369.9 2.9 copy.28
  374.7 3.2 copy.25
  378.0 6.5 fusion.34
  384.5 2.8 fusion.86
  387.4 2.9 convolution_add_fusion
  390.3 2.8 fusion.88
  393.2 3.1 convolution_subtract_fusion
  399.4 39.1 %collective-permute-done.4 = bf16[2,2,256,1024]{2,3,1,0:T(8,128)(2,1)} collective-permute-done((bf16[2,2,256,1024]{2,3,1,0:T(8,128)(2,1)}, bf16[2,2,256,1024]{2,3,1,0:T(8,128)(2,1)}, u32[]{:S(2)}, u32[]{:S(2)}) %collective-permute-start.4) | collective-permute-done | bytes 2097184 | tf_op jit(solution)/shard_map/ppermute | solution.py:15
  438.4 5.4 convert_bitcast_fusion.7
  445.5 38.9 %collective-permute-done.5 = bf16[2,2,256,1024]{2,3,1,0:T(8,128)(2,1)} collective-permute-done((bf16[2,2,256,1024]{2,3,1,0:T(8,128)(2,1)}, bf16[2,2,256,1024]{2,3,1,0:T(8,128)(2,1)}, u32[]{:S(2)}, u32[]{:S(2)}) %collective-permute-start.5) | collective-permute-done | bytes 2097184 | tf_op jit(solution)/shard_map/ppermute | solution.py:15
  484.4 5.4 convert_bitcast_fusion.5
  490.1 39.8 %collective-permute-done.6 = bf16[2,2,256,1024]{2,3,1,0:T(8,128)(2,1)} collective-permute-done((bf16[2,2,256,1024]{2,3,1,0:T(8,128)(2,1)S(1)}, bf16[2,2,256,1024]{2,3,1,0:T(8,128)(2,1)}, u32[]{:S(2)}, u32[]{:S(2)}) %collective-permute-start.6) | collective-permute-done | bytes 2097184 | tf_op jit(solution)/shard_map/ppermute | solution.py:15
  530.0 5.3 convert_bitcast_fusion.2
  538.9 31.6 %collective-permute-done.7 = bf16[2,2,256,1024]{2,3,1,0:T(8,128)(2,1)} collective-permute-done((bf16[2,2,256,1024]{2,3,1,0:T(8,128)(2,1)}, bf16[2,2,256,1024]{2,3,1,0:T(8,128)(2,1)}, u32[]{:S(2)}, u32[]{:S(2)}) %collective-permute-start.7) | collective-permute-done | bytes 2097184 | tf_op jit(solution)/shard_map/ppermute | solution.py:15
  576.0 3.3 copy-done.4
  581.9 3.7 collective-permute-start.9
  585.6 11.2 %collective-permute-done.8 = bf16[256,1024]{0,1:T(8,128)(2,1)S(1)} collective-permute-done((bf16[256,1024]{0,1:T(8,128)(2,1)S(1)}, bf16[256,1024]{0,1:T(8,128)(2,1)S(1)}, u32[]{:S(2)}, u32[]{:S(2)}) %collective-permute-start.8) | collective-permute-done | bytes 524320 | tf_op jit(solution)/shard_map/ppermute | solution.py:153
  597.8 5.8 collective-permute-start.11
  603.6 10.9 %collective-permute-done.10 = bf16[256,1024]{0,1:T(8,128)(2,1)S(1)} collective-permute-done((bf16[256,1024]{0,1:T(8,128)(2,1)S(1)}, bf16[256,1024]{0,1:T(8,128)(2,1)S(1)}, u32[]{:S(2)}, u32[]{:S(2)}) %collective-permute-start.10) | collective-permute-done | bytes 524320 | tf_op jit(solution)/shard_map/ppermute | solution.py:153
  615.3 5.9 collective-permute-start.13
  621.2 9.8 %collective-permute-done.12 = bf16[256,1024]{0,1:T(8,128)(2,1)S(1)} collective-permute-done((bf16[256,1024]{0,1:T(8,128)(2,1)S(1)}, bf16[256,1024]{0,1:T(8,128)(2,1)S(1)}, u32[]{:S(2)}, u32[]{:S(2)}) %collective-permute-start.12) | collective-permute-done | bytes 524320 | tf_op jit(solution)/shard_map/ppermute | solution.py:153
  634.9 5.4 collective-permute-start.15
  640.3 6.7 collective-permute-done.14
  647.0 18.2 %fusion = (f32[8,256]{1,0:T(8,128)S(1)}, f32[8,256,4096]{2,1,0:T(8,128)}) fusion(pred[256,4096]{1,0:T(8,128)(4,1)S(1)} %copy.31, bf16[4096,8,128]{0,2,1:T(8,128)(2,1)} %bitcast.290, bf16[256,1024]{1,0:T(8,128)(2,1)S(1)} %copy-done), kind=kOutput, calls=%fused_computation.4 | convolution fusion | flops 2172647424 | bytes 43524096 | tf_op jit(solution)/shard_map/thd,shd->hts/dot_general | solution.py:176
  665.2 5.3 collective-permute-start.17
  670.5 16.2 %fusion.1 = f32[8,256]{1,0:T(8,128)S(1)} fusion(f32[8,256,4096]{2,1,0:T(8,128)} %get-tuple-element.59, f32[8,256]{1,0:T(8,128)S(1)} %broadcast_maximum_fusion, pred[256,4096]{1,0:T(8,128)(4,1)S(1)} %copy.31), kind=kLoop, calls=%fused_computation.5 | loop fusion | flops 41940992 | bytes 34619392 | tf_op jit(solution)/shard_map/reduce_sum | solution.py:182
  691.4 5.3 collective-permute-start.19
  705.1 5.5 collective-permute-start.21
  719.1 6.0 collective-permute-done.22
  726.0 16.3 %divide_convert_fusion = bf16[256,8,128]{0,2,1:T(8,128)(2,1)S(1)} fusion(bf16[4096,8,128]{0,2,1:T(8,128)(2,1)} %bitcast.291, f32[8,256,4096]{2,1,0:T(8,128)} %get-tuple-element.59, f32[8,256]{1,0:T(8,128)S(1)} %broadcast_maximum_fusion, pred[256,4096]{1,0:T(8,128)(4,1)S(1)} %copy.31, f32[256,8]{0,1:T(8,128)S(1)} %bitcast.296), kind=kOutput, calls=%fused_computation.144 | convolution fusion | flops 2189950976 | bytes 43532288 | tf_op jit(solution)/shard_map/hts,shd->htd/dot_general | solution.py:183
  (134 shorter events, 67.1 us)
Async XLA Ops:
  7.2 639.8 %copy-start = (bf16[256,1024]{1,0:T(8,128)(2,1)S(1)}, bf16[256,1024]{1,0:T(8,128)(2,1)}, u32[]{:S(2)}) copy-start(bf16[256,1024]{1,0:T(8,128)(2,1)} %param.17) | copy-start | bytes 1572868
  7.2 246.4 %all-gather.3.cloned.1.call-start = ((), (), s32[]{:S(2)}) async-start(), calls=%async_computation | async-start | bytes 4456448 | tf_op jit(solution)/shard_map/all_gather | solution.py:200
  23.4 623.6 %all-gather.5.cloned.1.call-start = ((), (), s32[]{:S(2)}) async-start(), calls=%async_computation.1 | async-start | bytes 8912896 | tf_op jit(solution)/shard_map/all_gather | solution.py:136
  27.2 17.8 %collective-permute-start = (bf16[256,1024]{0,1:T(8,128)(2,1)S(1)}, bf16[256,1024]{0,1:T(8,128)(2,1)S(1)}, u32[]{:S(2)}, u32[]{:S(2)}) collective-permute-start(bf16[256,1024]{0,1:T(8,128)(2,1)S(1)} %get-tuple-element.36), channel_id=1, source_target_pairs={{0,64},{8,72},{16,80},{24,88},{32,96},{40,104},{48,112},{56,120},{... | collective-permute-start | bytes 1572872 | tf_op jit(solution)/shard_map/ppermute | solution.py:15
  30.5 14.7 %copy-start.7 = (f32[1,256,1024]{1,2,0:T(8,128)S(1)}, f32[1,256,1024]{1,2,0:T(8,128)}, u32[]{:S(2)}) copy-start(f32[1,256,1024]{1,2,0:T(8,128)} %get-tuple-element.35) | copy-start | bytes 3145732
  48.9 64.4 %collective-permute-start.1 = (bf16[2,2,256,1024]{2,3,1,0:T(8,128)(2,1)}, bf16[2,2,256,1024]{2,3,1,0:T(8,128)(2,1)}, u32[]{:S(2)}, u32[]{:S(2)}) collective-permute-start(bf16[2,2,256,1024]{2,3,1,0:T(8,128)(2,1)} %pad_maximum_fusion.2), channel_id=1, source_target_pairs={{0,32},{8,40},{16,48},{24,56},{32,0},{40,8},{48,16},{56,24},{64,96... | collective-permute-start | bytes 6291464 | tf_op jit(solution)/shard_map/ppermute | solution.py:15
  118.9 48.0 %collective-permute-start.2 = (bf16[2,2,256,1024]{2,3,1,0:T(8,128)(2,1)S(1)}, bf16[2,2,256,1024]{2,3,1,0:T(8,128)(2,1)}, u32[]{:S(2)}, u32[]{:S(2)}) collective-permute-start(bf16[2,2,256,1024]{2,3,1,0:T(8,128)(2,1)S(1)} %pad_maximum_fusion.3), channel_id=1, source_target_pairs={{0,16},{8,24},{16,0},{24,8},{32,48},{40,56},{48,32},{56,40},{64,80... | collective-permute-start | bytes 6291464 | tf_op jit(solution)/shard_map/ppermute | solution.py:15
  172.1 3.8 copy-start.16
  173.7 65.5 %collective-permute-start.3 = (bf16[2,2,256,1024]{2,3,1,0:T(8,128)(2,1)}, bf16[2,2,256,1024]{2,3,1,0:T(8,128)(2,1)}, u32[]{:S(2)}, u32[]{:S(2)}) collective-permute-start(bf16[2,2,256,1024]{2,3,1,0:T(8,128)(2,1)} %pad_maximum_fusion.4), channel_id=1, source_target_pairs={{0,8},{8,0},{16,24},{24,16},{32,40},{40,32},{48,56},{56,48},{64,72... | collective-permute-start | bytes 6291464 | tf_op jit(solution)/shard_map/ppermute | solution.py:15
  242.4 2.9 copy-start.1
  374.7 3.2 copy-start.2
  396.3 1.4 copy-start.3
  399.3 39.1 %collective-permute-start.4 = (bf16[2,2,256,1024]{2,3,1,0:T(8,128)(2,1)}, bf16[2,2,256,1024]{2,3,1,0:T(8,128)(2,1)}, u32[]{:S(2)}, u32[]{:S(2)}) collective-permute-start(bf16[2,2,256,1024]{2,3,1,0:T(8,128)(2,1)} %pad_maximum_fusion.5), channel_id=1, source_target_pairs={{0,8},{8,0},{16,24},{24,16},{32,40},{40,32},{48,56},{56,48},{64,72... | collective-permute-start | bytes 6291464 | tf_op jit(solution)/shard_map/ppermute | solution.py:15
  443.9 40.5 %copy-start.6 = (f32[2,256,1024]{1,2,0:T(8,128)S(1)}, f32[2,256,1024]{1,2,0:T(8,128)}, u32[]{:S(2)}) copy-start(f32[2,256,1024]{1,2,0:T(8,128)} %get-tuple-element.20) | copy-start | bytes 6291460
  445.4 38.9 %collective-permute-start.5 = (bf16[2,2,256,1024]{2,3,1,0:T(8,128)(2,1)}, bf16[2,2,256,1024]{2,3,1,0:T(8,128)(2,1)}, u32[]{:S(2)}, u32[]{:S(2)}) collective-permute-start(bf16[2,2,256,1024]{2,3,1,0:T(8,128)(2,1)} %pad_maximum_fusion.6), channel_id=1, source_target_pairs={{0,16},{8,24},{16,0},{24,8},{32,48},{40,56},{48,32},{56,40},{64,80... | collective-permute-start | bytes 6291464 | tf_op jit(solution)/shard_map/ppermute | solution.py:15
  490.0 40.0 %collective-permute-start.6 = (bf16[2,2,256,1024]{2,3,1,0:T(8,128)(2,1)S(1)}, bf16[2,2,256,1024]{2,3,1,0:T(8,128)(2,1)}, u32[]{:S(2)}, u32[]{:S(2)}) collective-permute-start(bf16[2,2,256,1024]{2,3,1,0:T(8,128)(2,1)S(1)} %pad_maximum_fusion.7), channel_id=1, source_target_pairs={{0,32},{8,40},{16,48},{24,56},{32,0},{40,8},{48,16},{56,24},{64,96... | collective-permute-start | bytes 6291464 | tf_op jit(solution)/shard_map/ppermute | solution.py:15
  536.8 33.7 %collective-permute-start.7 = (bf16[2,2,256,1024]{2,3,1,0:T(8,128)(2,1)}, bf16[2,2,256,1024]{2,3,1,0:T(8,128)(2,1)}, u32[]{:S(2)}, u32[]{:S(2)}) collective-permute-start(bf16[2,2,256,1024]{2,3,1,0:T(8,128)(2,1)} %pad_maximum_fusion.8), channel_id=1, source_target_pairs={{0,64},{8,72},{16,80},{24,88},{32,96},{40,104},{48,112},{56,120},{... | collective-permute-start | bytes 6291464 | tf_op jit(solution)/shard_map/ppermute | solution.py:15
  538.8 33.0 %copy-start.5 = (f32[2,256,1024]{1,2,0:T(8,128)S(1)}, f32[2,256,1024]{1,2,0:T(8,128)}, u32[]{:S(2)}) copy-start(f32[2,256,1024]{1,2,0:T(8,128)} %get-tuple-element.40) | copy-start | bytes 6291460
  574.2 1.1 copy-start.10
  574.2 1.1 copy-start.17
  575.3 39.2 %copy-start.18 = (s32[2,32]{1,0:T(2,128)S(1)}, s32[2,32]{1,0:T(2,128)}, u32[]{:S(2)}) copy-start(s32[2,32]{1,0:T(2,128)} %param.19) | copy-start | bytes 772
  576.0 3.3 copy-start.4
  579.3 2.6 copy-start.8
  579.3 17.6 %collective-permute-start.8 = (bf16[256,1024]{0,1:T(8,128)(2,1)S(1)}, bf16[256,1024]{0,1:T(8,128)(2,1)S(1)}, u32[]{:S(2)}, u32[]{:S(2)}) collective-permute-start(bf16[256,1024]{0,1:T(8,128)(2,1)S(1)} %get-tuple-element.8), channel_id=1, source_target_pairs={{0,8},{8,16},{16,24},{24,32},{32,40},{40,48},{48,56},{56,64},{64,7... | collective-permute-start | bytes 1572872 | tf_op jit(solution)/shard_map/ppermute | solution.py:153
  581.9 15.9 %collective-permute-start.9 = (bf16[256,1024]{0,1:T(8,128)(2,1)S(1)}, bf16[256,1024]{0,1:T(8,128)(2,1)S(1)}, u32[]{:S(2)}, u32[]{:S(2)}) collective-permute-start(bf16[256,1024]{0,1:T(8,128)(2,1)S(1)} %get-tuple-element.8), channel_id=1, source_target_pairs={{0,120},{8,0},{16,8},{24,16},{32,24},{40,32},{48,40},{56,48},{64,5... | collective-permute-start | bytes 1572872 | tf_op jit(solution)/shard_map/ppermute | solution.py:158
  596.8 6.8 copy-start.11
  596.8 17.7 %collective-permute-start.10 = (bf16[256,1024]{0,1:T(8,128)(2,1)S(1)}, bf16[256,1024]{0,1:T(8,128)(2,1)S(1)}, u32[]{:S(2)}, u32[]{:S(2)}) collective-permute-start(bf16[256,1024]{0,1:T(8,128)(2,1)S(1)} %collective-permute-done.8), channel_id=1, source_target_pairs={{0,8},{8,16},{16,24},{24,32},{32,40},{40,48},{48,56},{56,64},{64,7... | collective-permute-start | bytes 1572872 | tf_op jit(solution)/shard_map/ppermute | solution.py:153
  597.8 33.2 %copy-start.13 = (bf16[256,1024]{0,1:T(8,128)(2,1)}, bf16[256,1024]{0,1:T(8,128)(2,1)S(1)}, u32[]{:S(2)}) copy-start(bf16[256,1024]{0,1:T(8,128)(2,1)S(1)} %collective-permute-done.9) | copy-start | bytes 1572868
  597.8 17.5 %collective-permute-start.11 = (bf16[256,1024]{0,1:T(8,128)(2,1)S(1)}, bf16[256,1024]{0,1:T(8,128)(2,1)}, u32[]{:S(2)}, u32[]{:S(2)}) collective-permute-start(bf16[256,1024]{0,1:T(8,128)(2,1)S(1)} %collective-permute-done.9), channel_id=1, source_target_pairs={{0,120},{8,0},{16,8},{24,16},{32,24},{40,32},{48,40},{56,48},{64,5... | collective-permute-start | bytes 1572872 | tf_op jit(solution)/shard_map/ppermute | solution.py:158
  614.6 16.5 %copy-start.14 = (bf16[256,1024]{0,1:T(8,128)(2,1)}, bf16[256,1024]{0,1:T(8,128)(2,1)S(1)}, u32[]{:S(2)}) copy-start(bf16[256,1024]{0,1:T(8,128)(2,1)S(1)} %collective-permute-done.10) | copy-start | bytes 1572868
  614.6 16.5 %collective-permute-start.12 = (bf16[256,1024]{0,1:T(8,128)(2,1)S(1)}, bf16[256,1024]{0,1:T(8,128)(2,1)S(1)}, u32[]{:S(2)}, u32[]{:S(2)}) collective-permute-start(bf16[256,1024]{0,1:T(8,128)(2,1)S(1)} %collective-permute-done.10), channel_id=1, source_target_pairs={{0,8},{8,16},{16,24},{24,32},{32,40},{40,48},{48,56},{56,64},{64,7... | collective-permute-start | bytes 1572872 | tf_op jit(solution)/shard_map/ppermute | solution.py:153
  615.3 19.5 %collective-permute-start.13 = (bf16[256,1024]{0,1:T(8,128)(2,1)}, bf16[256,1024]{0,1:T(8,128)(2,1)}, u32[]{:S(2)}, u32[]{:S(2)}) collective-permute-start(bf16[256,1024]{0,1:T(8,128)(2,1)} %collective-permute-done.11), channel_id=1, source_target_pairs={{0,120},{8,0},{16,8},{24,16},{32,24},{40,32},{48,40},{56,48},{64,5... | collective-permute-start | bytes 1572872 | tf_op jit(solution)/shard_map/ppermute | solution.py:158
  631.0 15.9 %collective-permute-start.14 = (bf16[256,1024]{0,1:T(8,128)(2,1)S(1)}, bf16[256,1024]{0,1:T(8,128)(2,1)}, u32[]{:S(2)}, u32[]{:S(2)}) collective-permute-start(bf16[256,1024]{0,1:T(8,128)(2,1)S(1)} %collective-permute-done.12), channel_id=1, source_target_pairs={{0,8},{8,16},{16,24},{24,32},{32,40},{40,48},{48,56},{56,64},{64,7... | collective-permute-start | bytes 1572872 | tf_op jit(solution)/shard_map/ppermute | solution.py:153
  634.9 30.3 %collective-permute-start.15 = (bf16[256,1024]{0,1:T(8,128)(2,1)}, bf16[256,1024]{0,1:T(8,128)(2,1)}, u32[]{:S(2)}, u32[]{:S(2)}) collective-permute-start(bf16[256,1024]{0,1:T(8,128)(2,1)} %collective-permute-done.13), channel_id=1, source_target_pairs={{0,120},{8,0},{16,8},{24,16},{32,24},{40,32},{48,40},{56,48},{64,5... | collective-permute-start | bytes 1572872 | tf_op jit(solution)/shard_map/ppermute | solution.py:158
  647.0 23.5 %collective-permute-start.16 = (bf16[256,1024]{0,1:T(8,128)(2,1)}, bf16[256,1024]{0,1:T(8,128)(2,1)}, u32[]{:S(2)}, u32[]{:S(2)}) collective-permute-start(bf16[256,1024]{0,1:T(8,128)(2,1)} %collective-permute-done.14), channel_id=1, source_target_pairs={{0,8},{8,16},{16,24},{24,32},{32,40},{40,48},{48,56},{56,64},{64,7... | collective-permute-start | bytes 1572872 | tf_op jit(solution)/shard_map/ppermute | solution.py:153
  665.2 26.2 %collective-permute-start.17 = (bf16[256,1024]{0,1:T(8,128)(2,1)}, bf16[256,1024]{0,1:T(8,128)(2,1)}, u32[]{:S(2)}, u32[]{:S(2)}) collective-permute-start(bf16[256,1024]{0,1:T(8,128)(2,1)} %collective-permute-done.15), channel_id=1, source_target_pairs={{0,120},{8,0},{16,8},{24,16},{32,24},{40,32},{48,40},{56,48},{64,5... | collective-permute-start | bytes 1572872 | tf_op jit(solution)/shard_map/ppermute | solution.py:158
  670.5 28.1 %collective-permute-start.18 = (bf16[256,1024]{0,1:T(8,128)(2,1)}, bf16[256,1024]{0,1:T(8,128)(2,1)}, u32[]{:S(2)}, u32[]{:S(2)}) collective-permute-start(bf16[256,1024]{0,1:T(8,128)(2,1)} %collective-permute-done.16), channel_id=1, source_target_pairs={{0,8},{8,16},{16,24},{24,32},{32,40},{40,48},{48,56},{56,64},{64,7... | collective-permute-start | bytes 1572872 | tf_op jit(solution)/shard_map/ppermute | solution.py:153
  670.5 16.2 %copy-start.9 = (bf16[256,1024]{0,1:T(8,128)(2,1)S(1)}, bf16[256,1024]{0,1:T(8,128)(2,1)}, u32[]{:S(2)}) copy-start(bf16[256,1024]{0,1:T(8,128)(2,1)} %copy-done.8) | copy-start | bytes 1572868
  670.5 17.2 %copy-start.12 = (bf16[256,1024]{0,1:T(8,128)(2,1)S(1)}, bf16[256,1024]{0,1:T(8,128)(2,1)}, u32[]{:S(2)}) copy-start(bf16[256,1024]{0,1:T(8,128)(2,1)} %copy-done.11) | copy-start | bytes 1572868
  687.7 2.8 copy-start.15
  691.4 13.8 %collective-permute-start.19 = (bf16[256,1024]{0,1:T(8,128)(2,1)}, bf16[256,1024]{0,1:T(8,128)(2,1)S(1)}, u32[]{:S(2)}, u32[]{:S(2)}) collective-permute-start(bf16[256,1024]{0,1:T(8,128)(2,1)} %collective-permute-done.17), channel_id=1, source_target_pairs={{0,120},{8,0},{16,8},{24,16},{32,24},{40,32},{48,40},{56,48},{64,5... | collective-permute-start | bytes 1572872 | tf_op jit(solution)/shard_map/ppermute | solution.py:158
  698.6 14.0 %collective-permute-start.20 = (bf16[256,1024]{0,1:T(8,128)(2,1)}, bf16[256,1024]{0,1:T(8,128)(2,1)S(1)}, u32[]{:S(2)}, u32[]{:S(2)}) collective-permute-start(bf16[256,1024]{0,1:T(8,128)(2,1)} %collective-permute-done.18), channel_id=1, source_target_pairs={{0,8},{8,16},{16,24},{24,32},{32,40},{40,48},{48,56},{56,64},{64,7... | collective-permute-start | bytes 1572872 | tf_op jit(solution)/shard_map/ppermute | solution.py:153
  705.1 13.0 %collective-permute-start.21 = (bf16[256,1024]{0,1:T(8,128)(2,1)S(1)}, bf16[256,1024]{0,1:T(8,128)(2,1)S(1)}, u32[]{:S(2)}, u32[]{:S(2)}) collective-permute-start(bf16[256,1024]{0,1:T(8,128)(2,1)S(1)} %collective-permute-done.19), channel_id=1, source_target_pairs={{0,120},{8,0},{16,8},{24,16},{32,24},{40,32},{48,40},{56,48},{64,5... | collective-permute-start | bytes 1572872 | tf_op jit(solution)/shard_map/ppermute | solution.py:158
  712.6 12.5 %collective-permute-start.22 = (bf16[256,1024]{0,1:T(8,128)(2,1)S(1)}, bf16[256,1024]{0,1:T(8,128)(2,1)S(1)}, u32[]{:S(2)}, u32[]{:S(2)}) collective-permute-start(bf16[256,1024]{0,1:T(8,128)(2,1)S(1)} %collective-permute-done.20), channel_id=1, source_target_pairs={{0,8},{8,16},{16,24},{24,32},{32,40},{40,48},{48,56},{56,64},{64,7... | collective-permute-start | bytes 1572872 | tf_op jit(solution)/shard_map/ppermute | solution.py:153
Sparse Core Ops, SparseCore 0:
  23.5 73.5 all-gather.2
  176.0 90.3 all-gather.4
